TPU v7x, 512 devices: a whole 4x8x8 slice. The times are simulated.
512 devices in a mesh: dp: 4 (over z_lo, core), ctx: 128 (over x, y, z_hi).
Axes of the slice: x: 4, y: 8, z: 8 (z_hi: 4, z_lo: 2; z = z_hi * 2 + z_lo), core: 2. Of those that a mesh axis runs over, the one named last changes fastest.
Arguments:
- query: bfloat16 [4, 32768, 1024], P('dp', 'ctx'), may hold values from -150 to 150
- key: bfloat16 [4, 32768, 1024], P('dp', 'ctx'), may hold values from -3 to 3
- value: bfloat16 [4, 32768, 1024], P('dp', 'ctx'), may hold values from -6 to 6
- grad_out: bfloat16 [4, 32768, 1024], P('dp', 'ctx'), may hold values from -30 to 30
- clause: int32 [4, 32768], P('dp', 'ctx'), may hold values from 0 to 2047, never falling along the last dimension, each value on 1 to 48 neighbouring positions
- bias_table: float32 [32, 2], replicated, may hold values from -1.5 to 1.5
Outputs:
- attended: bfloat16 [4, 32768, 1024], P('dp', 'ctx')
- query_gradient: bfloat16 [4, 32768, 1024], P('dp', 'ctx')
- key_gradient: bfloat16 [4, 32768, 1024], P('dp', 'ctx')
- value_gradient: bfloat16 [4, 32768, 1024], P('dp', 'ctx')
- bias_grad: float32 [32, 2], replicated
Inputs may be any that keep to these rules, and one draw needn't show every extreme that they name: Clause ids never fall along a document; a clause holds 1 to 48 tokens, and some clause holds exactly 48.
All inputs are finite; a program needn't handle non-finite values.
Results may differ from a plain program's by a relative error of at most 0.009.
Values may be sent and summed in bfloat16 or wider, within the bound.
No kernel may reach another device: no remote copies, remote signals or barrier semaphores. Data moves between devices by JAX's collectives and lax.ppermute only.
A program may use at most 128 MiB of HBM per device.

v0:
```python
import jax
import jax.numpy as jnp
from jax import lax
from jax.sharding import PartitionSpec as P

HEADS = 8
WINDOW = 512
BUCKETS = 32
DILATION_FIRST = 1
DILATION_SECOND = 8
DILATION_THIRD = 32


def swapped(block, axis, bit):
    count = lax.axis_size(axis)
    route = []
    for low in range(count):
        high = low | 1 << bit
        if high != low and high < count:
            route += [(low, high), (high, low)]
    return lax.ppermute(block, axis, route)


def shifted(value, axis, steps):
    count = lax.axis_size(axis)
    leading, last = (max(0, -steps), min(count, count - steps))
    return lax.ppermute(value, axis, [(source, source + steps) for source in range(leading, last)])


def with_halo(shard, sides, width):
    for axis, dim in sides:
        size, length = (lax.axis_size(axis), shard.shape[dim])
        up = [(i, (i + 1) % size) for i in range(size - 1)]
        down = [(j, i) for i, j in up]
        last = lax.slice_in_dim(shard, length - width, length, axis=dim)
        leading = lax.slice_in_dim(shard, 0, width, axis=dim)
        before = lax.ppermute(last, axis, up)
        after = lax.ppermute(leading, axis, down)
        shard = jnp.concatenate([before, shard, after], axis=dim)
    return shard


def sample_rows(matrix, initial_flag, dilation_rate):
    count = matrix.shape[0] // dilation_rate
    head_dim = matrix.shape[1] // HEADS
    grid = matrix.reshape(count, dilation_rate, HEADS, head_dim)
    return jnp.concatenate(
        [grid[:, 0, initial_flag], grid[:, dilation_rate // 2, initial_flag + 1]], axis=1
    )


def spread_rows(sampled, dilation_rate):
    count = sampled.shape[0]
    grid = jnp.zeros((count, dilation_rate) + sampled.shape[1:], sampled.dtype)
    grid = grid.at[:, 0, 0].set(sampled[:, 0]).at[:, dilation_rate // 2, 1].set(sampled[:, 1])
    return grid.reshape((count * dilation_rate,) + sampled.shape[1:])


def upper_half(bit):
    index = lax.axis_index("ctx")
    return index // 2**bit % 2 == 1


def double_rows(block, bits):
    for bit in range(bits):
        other = swapped(block, "ctx", bit)
        block = jnp.where(
            upper_half(bit),
            jnp.concatenate([other, block], axis=0),
            jnp.concatenate([block, other], axis=0),
        )
    return block


def halve_sums(block, bits):
    for bit in reversed(range(bits)):
        half = block.shape[0] // 2
        lower, higher = (block[:half], block[half:])
        upper = upper_half(bit)
        outgoing = jnp.where(upper, lower, higher)
        staying = jnp.where(upper, higher, lower)
        block = staying + swapped(outgoing.astype(jnp.bfloat16), "ctx", bit).astype(outgoing.dtype)
    return block


def span_rows(block, bits):
    return double_rows(block, bits)


def span_sums(block, bits):
    return halve_sums(block, bits)


def rows_side(score_matrix, every_key_rows, every_value_rows, gradient_list, score_scale):
    top = jnp.max(score_matrix, axis=-1, keepdims=True)
    raised = jnp.exp(score_matrix - top)
    totals = jnp.sum(raised, axis=-1, keepdims=True)
    shares = raised / totals
    softmax_weights = shares.astype(jnp.bfloat16)
    attended = jnp.einsum(
        "ezb,beo->zeo", softmax_weights, every_value_rows, preferred_element_type=jnp.float32
    )
    weight_gradient = jnp.einsum(
        "wvx,yvx->vwy", gradient_list, every_value_rows, preferred_element_type=jnp.float32
    )
    delta = jnp.sum(shares * weight_gradient, axis=-1, keepdims=True)
    logit_grads = shares * (weight_gradient - delta)
    score_gradient = logit_grads.astype(jnp.bfloat16)
    query_gradient = (
        jnp.einsum(
            "ezb,beo->zeo", score_gradient, every_key_rows, preferred_element_type=jnp.float32
        )
        * score_scale
    )
    return (
        attended,
        query_gradient,
        softmax_weights,
        score_gradient,
        logit_grads,
        top,
        totals,
        delta,
    )


def keys_side(softmax_weights, score_gradient, query_matrix, gradient_list, score_scale):
    key_gradient = (
        jnp.einsum("vjb,jvw->bvw", score_gradient, query_matrix, preferred_element_type=jnp.float32)
        * score_scale
    )
    value_gradient = jnp.einsum(
        "vjb,jvw->bvw", softmax_weights, gradient_list, preferred_element_type=jnp.float32
    )
    return (key_gradient, value_gradient)


def bucket_lookup(bucket, table):
    running = jnp.zeros((table.shape[1],) + bucket.shape, jnp.float32)
    for level in range(BUCKETS):
        running = jnp.where(bucket[None] == level, table[level][:, None, None], running)
    return running


def bucket_sums(bucket, logit_grads):
    totals = [
        jnp.sum(jnp.where(bucket[None] == level, logit_grads, 0.0), axis=(1, 2))
        for level in range(BUCKETS)
    ]
    return jnp.stack(totals, axis=0)


def pass_rim(rim, offset):
    return shifted(rim.astype(jnp.bfloat16), "ctx", offset).astype(rim.dtype)


def band_part(query_rows, key_rows, value_rows, grad_rows, clause_rows, table, score_scale):
    rows, width = query_rows.shape
    head_dim = width // HEADS
    wide = 2 * head_dim
    half = WINDOW // 2
    pair_rows = jnp.concatenate([key_rows[:, :wide], value_rows[:, :wide]], axis=1)
    extended, extended_clause = (
        with_halo(pair_rows, (("ctx", 0),), half),
        with_halo(clause_rows, (("ctx", 0),), half),
    )
    reach = rows + 2 * half
    nearby_key_rows = extended[:, :wide].reshape(reach, 2, head_dim)
    values_near = extended[:, wide:].reshape(reach, 2, head_dim)
    query_matrix = query_rows[:, :wide].reshape(rows, 2, head_dim)
    gradient_list = grad_rows[:, :wide].reshape(rows, 2, head_dim)
    start = lax.axis_index("ctx") * rows
    length = rows * lax.axis_size("ctx")
    local_query = jnp.arange(rows)[:, None]
    local_key = jnp.arange(reach)[None, :] - half
    global_key = start + local_key
    allowed = (jnp.abs(local_query - local_key) < half) & (global_key >= 0) & (global_key < length)
    bucket = jnp.minimum(jnp.abs(clause_rows[:, None] - extended_clause[None, :]), BUCKETS - 1)
    score_matrix = (
        jnp.einsum(
            "wvx,yvx->vwy", query_matrix, nearby_key_rows, preferred_element_type=jnp.float32
        )
        * score_scale
    )
    score_matrix = jnp.where(allowed[None], score_matrix + bucket_lookup(bucket, table), -jnp.inf)
    attended, query_gradient, softmax_weights, score_gradient, logit_grads, top, totals, delta = (
        rows_side(score_matrix, nearby_key_rows, values_near, gradient_list, score_scale)
    )
    key_gradient, value_gradient = keys_side(
        softmax_weights, score_gradient, query_matrix, gradient_list, score_scale
    )
    sums = jnp.concatenate(
        [key_gradient.reshape(reach, wide), value_gradient.reshape(reach, wide)], axis=1
    )
    own = sums[half : half + rows]
    from_next = pass_rim(sums[:half], -1)
    from_prev = pass_rim(sums[half + rows :], 1)
    own = own.at[rows - half :].add(from_next).at[:half].add(from_prev)
    own_key = own[:, :wide].reshape(rows, 2, head_dim)
    own_value = own[:, wide:].reshape(rows, 2, head_dim)
    return (attended, query_gradient, own_key, own_value, bucket_sums(bucket, logit_grads))


def dilated(
    query_rows, key_rows, value_rows, grad_rows, initial_flag, dilation_rate, bits, score_scale
):
    head_dim = query_rows.shape[1] // HEADS
    wide = 2 * head_dim
    picked_query = sample_rows(query_rows, initial_flag, dilation_rate)
    picked_key = sample_rows(key_rows, initial_flag, dilation_rate)
    picked_value = sample_rows(value_rows, initial_flag, dilation_rate)
    picked_grad = sample_rows(grad_rows, initial_flag, dilation_rate)
    count = picked_query.shape[0]
    gathered = span_rows(jnp.concatenate([picked_key, picked_value], axis=1), bits)
    gathered_rows = gathered.shape[0]
    every_key_rows = gathered[:, :wide].reshape(gathered_rows, 2, head_dim)
    every_value_rows = gathered[:, wide:].reshape(gathered_rows, 2, head_dim)
    query_matrix = picked_query.reshape(count, 2, head_dim)
    gradient_list = picked_grad.reshape(count, 2, head_dim)
    score_matrix = (
        jnp.einsum("wvx,yvx->vwy", query_matrix, every_key_rows, preferred_element_type=jnp.float32)
        * score_scale
    )
    attended, query_gradient, softmax_weights, score_gradient, logit_grads, top, totals, delta = (
        rows_side(score_matrix, every_key_rows, every_value_rows, gradient_list, score_scale)
    )
    key_gradient, value_gradient = keys_side(
        softmax_weights, score_gradient, query_matrix, gradient_list, score_scale
    )
    partial_sums = jnp.concatenate(
        [key_gradient.reshape(gathered_rows, wide), value_gradient.reshape(gathered_rows, wide)],
        axis=1,
    )
    own = span_sums(partial_sums, bits)
    own_key = own[:, :wide].reshape(count, 2, head_dim)
    own_value = own[:, wide:].reshape(count, 2, head_dim)
    return (
        spread_rows(attended, dilation_rate),
        spread_rows(query_gradient, dilation_rate),
        spread_rows(own_key, dilation_rate),
        spread_rows(own_value, dilation_rate),
    )


def shards(query, key, value, grad_out, clause, bias_table):
    query_rows = query[0]
    key_rows = key[0]
    value_rows = value[0]
    grad_rows = grad_out[0]
    clause_rows = clause[0]
    rows, width = query_rows.shape
    head_dim = width // HEADS
    score_scale = head_dim ** (-0.5)
    bucket_bit_count = lax.axis_size("ctx").bit_length() - 1
    band = band_part(
        query_rows, key_rows, value_rows, grad_rows, clause_rows, bias_table, score_scale
    )
    pieces = [band[:4]]
    for initial_flag, dilation_rate, bits in (
        (2, DILATION_FIRST, max(bucket_bit_count - 5, 1)),
        (4, DILATION_SECOND, bucket_bit_count - 2),
        (6, DILATION_THIRD, bucket_bit_count),
    ):
        pieces.append(
            dilated(
                query_rows,
                key_rows,
                value_rows,
                grad_rows,
                initial_flag,
                dilation_rate,
                bits,
                score_scale,
            )
        )
    bias_grad = lax.psum(band[4], ("dp", "ctx"))
    joined = [
        jnp.concatenate([piece[slot] for piece in pieces], axis=1)
        .reshape(1, rows, width)
        .astype(jnp.bfloat16)
        for slot in range(4)
    ]
    return (joined[0], joined[1], joined[2], joined[3], bias_grad)


def solution(mesh):
    in_specs = (
        P("dp", "ctx", None),
        P("dp", "ctx", None),
        P("dp", "ctx", None),
        P("dp", "ctx", None),
        P("dp", "ctx"),
        P(),
    )
    out_specs = (
        P("dp", "ctx", None),
        P("dp", "ctx", None),
        P("dp", "ctx", None),
        P("dp", "ctx", None),
        P(),
    )
    return jax.shard_map(shards, mesh=mesh, in_specs=in_specs, out_specs=out_specs, check_vma=False)
```

profile of v0, /device:TPU:6, one launch (start us, length us, event | category | flops | bytes accessed | tf_op | source)
XLA Modules:
  0.0 409.0 jit_solution(8975889016358861328)
XLA Ops:
  0.6 14.2 %collective-permute-start.3 = (s32[256]{0:T(256)}, s32[256]{0:T(256)}, u32[]{:S(2)}, u32[]{:S(2)}) collective-permute-start(s32[256]{0:T(256)} %bitcast.409), channel_id=1, source_target_pairs={{1,0},{2,1},{3,2},{4,3},{5,4},{6,5},{7,6},{8,7},{9,8},{10,9},{11,1... | collective-permute-start | bytes 3080 | tf_op jit(solution)/shard_map/ppermute | solution.py:38
  14.9 1.9 collective-permute-start.2
  19.1 9.0 %collective-permute-start.1 = (bf16[256,512]{0,1:T(8,128)(2,1)}, bf16[256,512]{0,1:T(8,128)(2,1)}, u32[]{:S(2)}, u32[]{:S(2)}) collective-permute-start(bf16[256,512]{0,1:T(8,128)(2,1)} %pad_maximum_fusion.9), channel_id=1, source_target_pairs={{1,0},{2,1},{3,2},{4,3},{5,4},{6,5},{7,6},{8,7},{9,8},{10,9},{11,1... | collective-permute-start | bytes 786440 | tf_op jit(solution)/shard_map/ppermute | solution.py:38
  46.3 4.8 %collective-permute-start.6 = (bf16[32,512]{1,0:T(8,128)(2,1)S(1)}, bf16[32,512]{1,0:T(8,128)(2,1)S(1)}, u32[]{:S(2)}, u32[]{:S(2)}) collective-permute-start(bf16[32,512]{1,0:T(8,128)(2,1)S(1)} %pad_maximum_fusion.21), channel_id=1, source_target_pairs={{0,1},{1,0},{2,3},{3,2},{4,5},{5,4},{6,7},{7,6},{8,9},{9,8},{10,11... | collective-permute-start | bytes 98312 | tf_op jit(solution)/shard_map/ppermute | solution.py:21
  53.8 4.0 collective-permute-start.12
  58.5 5.1 %collective-permute-done.12 = bf16[16,512]{1,0:T(8,128)(2,1)S(1)} collective-permute-done((bf16[16,512]{1,0:T(8,128)(2,1)S(1)}, bf16[16,512]{1,0:T(8,128)(2,1)S(1)}, u32[]{:S(2)}, u32[]{:S(2)}) %collective-permute-start.12) | collective-permute-done | bytes 16416 | tf_op jit(solution)/shard_map/ppermute | solution.py:21
  65.6 5.4 %collective-permute-start.7 = (bf16[64,512]{1,0:T(8,128)(2,1)S(1)}, bf16[64,512]{1,0:T(8,128)(2,1)S(1)}, u32[]{:S(2)}, u32[]{:S(2)}) collective-permute-start(bf16[64,512]{1,0:T(8,128)(2,1)S(1)} %maximum_select_fusion.10), channel_id=1, source_target_pairs={{0,2},{2,0},{1,3},{3,1},{4,6},{6,4},{5,7},{7,5},{8,10},{10,8},{9,1... | collective-permute-start | bytes 196616 | tf_op jit(solution)/shard_map/ppermute | solution.py:21
  71.1 6.8 %collective-permute-start.14 = (bf16[64,512]{1,0:T(8,128)(2,1)S(1)}, bf16[64,512]{1,0:T(8,128)(2,1)S(1)}, u32[]{:S(2)}, u32[]{:S(2)}) collective-permute-start(bf16[64,512]{1,0:T(8,128)(2,1)S(1)} %maximum_select_fusion.11), channel_id=1, source_target_pairs={{0,8},{8,0},{1,9},{9,1},{2,10},{10,2},{3,11},{11,3},{4,12},{12,4},... | collective-permute-start | bytes 196616 | tf_op jit(solution)/shard_map/ppermute | solution.py:21
  80.6 4.3 %collective-permute-start.15 = (bf16[128,512]{1,0:T(8,128)(2,1)S(1)}, bf16[128,512]{1,0:T(8,128)(2,1)S(1)}, u32[]{:S(2)}, u32[]{:S(2)}) collective-permute-start(bf16[128,512]{1,0:T(8,128)(2,1)S(1)} %maximum_select_fusion.9), channel_id=1, source_target_pairs={{0,16},{16,0},{1,17},{17,1},{2,18},{18,2},{3,19},{19,3},{4,20},{20... | collective-permute-start | bytes 393224 | tf_op jit(solution)/shard_map/ppermute | solution.py:21
  84.9 4.9 %fusion.56 = (pred[256,768]{0,1:T(8,128)(4,1)S(1)}, pred[256,768]{0,1:T(8,128)(4,1)S(1)}, pred[256,768]{0,1:T(8,128)(4,1)S(1)}, pred[256,768]{0,1:T(8,128)(4,1)S...) fusion(s32[768]{0:T(1024)S(1)} %pad_add_fusion, ...), kind=kLoop, calls=%fused_computation.134 | loop fusion | flops 6881280 | bytes 6295552 | tf_op jit(solution)/shard_map/eq | solution.py:141
  90.2 3.0 collective-permute-start.9
  93.6 7.5 %collective-permute-start.16 = (bf16[256,512]{1,0:T(8,128)(2,1)S(1)}, bf16[256,512]{1,0:T(8,128)(2,1)}, u32[]{:S(2)}, u32[]{:S(2)}) collective-permute-start(bf16[256,512]{1,0:T(8,128)(2,1)S(1)} %maximum_select_fusion.7), channel_id=1, source_target_pairs={{0,32},{32,0},{1,33},{33,1},{2,34},{34,2},{3,35},{35,3},{4,36},{36... | collective-permute-start | bytes 786440 | tf_op jit(solution)/shard_map/ppermute | solution.py:21
  103.5 5.7 %fusion.9 = f32[2,256,768]{1,2,0:T(8,128)S(1)} fusion(bf16[768,2,128]{0,2,1:T(8,128)(2,1)S(1)} %bitcast.347, bf16[256,2,128]{0,2,1:T(8,128)(2,1)S(1)} %bitcast.361, f32[2]{0:T(128)S(1)} %copy-done.182, f32[2]{0:T(128)S(1)} %copy-done.183, f32[2]{0:T(128)S(1)} %copy-done.121, f32[2]{0:T(128)S(1)} %copy-done.122, f32[2]{0:T(128)S(1)} %copy-done.123, ...), kind=kOutput, calls=%fused_computation.25 | convolution fusion | flops 114425856 | bytes 8585472 | tf_op jit(solution)/shard_map/wvx,yvx->vwy/dot_general | solution.py:180
  110.9 2.5 fusion.68
  115.8 5.5 %select_reduce_fusion = (f32[2]{0:T(128)}, f32[2]{0:T(128)}, f32[2]{0:T(128)}, f32[2]{0:T(128)}, f32[2]{0:T(128)}, /*index=5*/f32[2]{0:T(128)}, f32[2]{0:T(128)}...) fusion(pred[256,768]{0,1:T(8,128)(4,1)S(1)} %copy-done.39, ...), kind=kLoop, calls=%fused_computation.26 | loop fusion | flops 15335388 | bytes 8261776 | tf_op jit(solution)/shard_map/reduce_sum | solution.py:147
  121.4 4.4 %select_reduce_fusion.18 = (f32[2]{0:T(128)}, f32[2]{0:T(128)}, f32[2]{0:T(128)}, f32[2]{0:T(128)}, f32[2]{0:T(128)}, /*index=5*/f32[2]{0:T(128)}, f32[2]{0:T(12...) fusion(f32[2,256,768]{1,2,0:T(8,128)S(1)} %get-tuple-element.442, ...), kind=kLoop, calls=%fused_computation.44 | loop fusion | flops 11010020 | bytes 4325488 | tf_op jit(solution)/shard_map/reduce_sum | solution.py:147
  128.5 3.1 fusion.15
  131.5 5.1 %collective-permute-start.18 = (bf16[256,512]{0,1:T(8,128)(2,1)}, bf16[256,512]{0,1:T(8,128)(2,1)}, u32[]{:S(2)}, u32[]{:S(2)}) collective-permute-start(bf16[256,512]{0,1:T(8,128)(2,1)} %get-tuple-element.449), channel_id=1, source_target_pairs={{1,0},{2,1},{3,2},{4,3},{5,4},{6,5},{7,6},{8,7},{9,8},{10,9},{11,1... | collective-permute-start | bytes 786440 | tf_op jit(solution)/shard_map/ppermute | solution.py:27
  139.7 4.6 %collective-permute-start.5 = (bf16[512,512]{0,1:T(8,128)(2,1)S(1)}, bf16[512,512]{0,1:T(8,128)(2,1)}, u32[]{:S(2)}, u32[]{:S(2)}) collective-permute-start(bf16[512,512]{0,1:T(8,128)(2,1)S(1)} %maximum_select_fusion.3), channel_id=1, source_target_pairs={{0,2},{2,0},{1,3},{3,1},{4,6},{6,4},{5,7},{7,5},{8,10},{10,8},{9,1... | collective-permute-start | bytes 1572872 | tf_op jit(solution)/shard_map/ppermute | solution.py:21
  147.5 111.7 %psum.7 = f32[32,2]{0,1:T(2,128)} all-reduce(f32[32,2]{0,1:T(2,128)S(1)} %stack.131), channel_id=1, replica_groups=mesh['dp'=4,'ctx'=128] {'dp','ctx'}, use_global_device_ids=true, to_apply=%region_44.45 | all-reduce | flops 64 | bytes 512 | tf_op jit(solution)/shard_map/psum | solution.py:276
  260.3 4.0 collective-permute-start.10
  264.3 2.0 maximum_select_fusion.5
  266.3 4.6 %collective-permute-start.17 = (bf16[512,512]{1,0:T(8,128)(2,1)}, bf16[512,512]{1,0:T(8,128)(2,1)}, u32[]{:S(2)}, u32[]{:S(2)}) collective-permute-start(bf16[512,512]{1,0:T(8,128)(2,1)} %maximum_select_fusion.5), channel_id=1, source_target_pairs={{0,64},{64,0},{1,65},{65,1},{2,66},{66,2},{3,67},{67,3},{4,68},{68... | collective-permute-start | bytes 1572872 | tf_op jit(solution)/shard_map/ppermute | solution.py:21
  275.1 2.1 fusion.133
  279.9 2.5 multiply_reduce_fusion
  284.7 4.5 %collective-permute-start.20 = (bf16[512,512]{0,1:T(8,128)(2,1)}, bf16[512,512]{0,1:T(8,128)(2,1)}, u32[]{:S(2)}, u32[]{:S(2)}) collective-permute-start(bf16[512,512]{0,1:T(8,128)(2,1)} %select_convert_fusion.2), channel_id=1, source_target_pairs={{0,2},{2,0},{1,3},{3,1},{4,6},{6,4},{5,7},{7,5},{8,10},{10,8},{9,1... | collective-permute-start | bytes 1572872 | tf_op jit(solution)/shard_map/ppermute | solution.py:21
  302.2 4.3 %collective-permute-start.22 = (bf16[512,512]{1,0:T(8,128)(2,1)}, bf16[512,512]{1,0:T(8,128)(2,1)}, u32[]{:S(2)}, u32[]{:S(2)}) collective-permute-start(bf16[512,512]{1,0:T(8,128)(2,1)} %select_convert_fusion.1), channel_id=1, source_target_pairs={{0,16},{16,0},{1,17},{17,1},{2,18},{18,2},{3,19},{19,3},{4,20},{20... | collective-permute-start | bytes 1572872 | tf_op jit(solution)/shard_map/ppermute | solution.py:21
  309.4 2.0 copy.639
  313.0 2.0 copy.636
  320.9 2.5 copy.675
  324.8 2.6 copy.674
  327.4 2.5 select_convert_fusion
  329.9 4.6 %collective-permute-start.27 = (bf16[512,512]{1,0:T(8,128)(2,1)}, bf16[512,512]{1,0:T(8,128)(2,1)}, u32[]{:S(2)}, u32[]{:S(2)}) collective-permute-start(bf16[512,512]{1,0:T(8,128)(2,1)} %select_convert_fusion), channel_id=1, source_target_pairs={{0,64},{64,0},{1,65},{65,1},{2,66},{66,2},{3,67},{67,3},{4,68},{68... | collective-permute-start | bytes 1572872 | tf_op jit(solution)/shard_map/ppermute | solution.py:21
  336.3 2.0 copy.717
  338.3 2.0 copy.718
  342.1 2.3 collective-permute-start.21
  345.7 2.2 collective-permute-start.23
  351.2 6.0 %collective-permute-done.21 = bf16[256,512]{0,1:T(8,128)(2,1)S(1)} collective-permute-done((bf16[256,512]{0,1:T(8,128)(2,1)S(1)}, bf16[256,512]{0,1:T(8,128)(2,1)S(1)}, u32[]{:S(2)}, u32[]{:S(2)}) %collective-permute-start.21) | collective-permute-done | bytes 262176 | tf_op jit(solution)/shard_map/ppermute | solution.py:21
  361.5 6.6 %collective-permute-start.29 = (bf16[128,512]{1,0:T(8,128)(2,1)S(1)}, bf16[128,512]{1,0:T(8,128)(2,1)S(1)}, u32[]{:S(2)}, u32[]{:S(2)}) collective-permute-start(bf16[128,512]{1,0:T(8,128)(2,1)S(1)} %select_convert_fusion.6), channel_id=1, source_target_pairs={{0,16},{16,0},{1,17},{17,1},{2,18},{18,2},{3,19},{19,3},{4,20},{20... | collective-permute-start | bytes 393224 | tf_op jit(solution)/shard_map/ppermute | solution.py:21
  368.2 4.5 %collective-permute-start.25 = (bf16[64,512]{1,0:T(8,128)(2,1)S(1)}, bf16[64,512]{1,0:T(8,128)(2,1)S(1)}, u32[]{:S(2)}, u32[]{:S(2)}) collective-permute-start(bf16[64,512]{1,0:T(8,128)(2,1)S(1)} %select_convert_fusion.9), channel_id=1, source_target_pairs={{0,2},{2,0},{1,3},{3,1},{4,6},{6,4},{5,7},{7,5},{8,10},{10,8},{9,1... | collective-permute-start | bytes 196616 | tf_op jit(solution)/shard_map/ppermute | solution.py:21
  372.9 6.8 %collective-permute-start.30 = (bf16[64,512]{1,0:T(8,128)(2,1)S(1)}, bf16[64,512]{1,0:T(8,128)(2,1)S(1)}, u32[]{:S(2)}, u32[]{:S(2)}) collective-permute-start(bf16[64,512]{1,0:T(8,128)(2,1)S(1)} %select_convert_fusion.8), channel_id=1, source_target_pairs={{0,8},{8,0},{1,9},{9,1},{2,10},{10,2},{3,11},{11,3},{4,12},{12,4},... | collective-permute-start | bytes 196616 | tf_op jit(solution)/shard_map/ppermute | solution.py:21
  379.7 4.5 %collective-permute-start.26 = (bf16[32,512]{1,0:T(8,128)(2,1)S(1)}, bf16[32,512]{1,0:T(8,128)(2,1)S(1)}, u32[]{:S(2)}, u32[]{:S(2)}) collective-permute-start(bf16[32,512]{1,0:T(8,128)(2,1)S(1)} %select_convert_fusion.11), channel_id=1, source_target_pairs={{0,1},{1,0},{2,3},{3,2},{4,5},{5,4},{6,7},{7,6},{8,9},{9,8},{10,11... | collective-permute-start | bytes 98312 | tf_op jit(solution)/shard_map/ppermute | solution.py:21
  384.4 3.0 collective-permute-start.31
  387.5 2.7 collective-permute-done.31
  390.2 5.2 %collective-permute-start.32 = (bf16[16,512]{1,0:T(8,128)(2,1)S(1)}, bf16[16,512]{1,0:T(8,128)(2,1)S(1)}, u32[]{:S(2)}, u32[]{:S(2)}) collective-permute-start(bf16[16,512]{1,0:T(8,128)(2,1)S(1)} %select_convert_fusion.12), channel_id=1, source_target_pairs={{0,2},{2,0},{1,3},{3,1},{4,6},{6,4},{5,7},{7,5},{8,10},{10,8},{9,1... | collective-permute-start | bytes 49160 | tf_op jit(solution)/shard_map/ppermute | solution.py:21
  395.5 4.3 %collective-permute-done.32 = bf16[16,512]{1,0:T(8,128)(2,1)S(1)} collective-permute-done((bf16[16,512]{1,0:T(8,128)(2,1)S(1)}, bf16[16,512]{1,0:T(8,128)(2,1)S(1)}, u32[]{:S(2)}, u32[]{:S(2)}) %collective-permute-start.32) | collective-permute-done | bytes 16416 | tf_op jit(solution)/shard_map/ppermute | solution.py:21
  399.8 2.9 collective-permute-start.33
  403.2 3.0 collective-permute-done.33
  (628 shorter events, 92.7 us)
Async XLA Ops:
  0.6 51.3 %collective-permute-start.3 = (s32[256]{0:T(256)}, s32[256]{0:T(256)}, u32[]{:S(2)}, u32[]{:S(2)}) collective-permute-start(s32[256]{0:T(256)} %bitcast.409), channel_id=1, source_target_pairs={{1,0},{2,1},{3,2},{4,3},{5,4},{6,5},{7,6},{8,7},{9,8},{10,9},{11,1... | collective-permute-start | bytes 3080 | tf_op jit(solution)/shard_map/ppermute | solution.py:38
  14.9 38.9 %collective-permute-start.2 = (s32[256]{0:T(256)}, s32[256]{0:T(256)}, u32[]{:S(2)}, u32[]{:S(2)}) collective-permute-start(s32[256]{0:T(256)} %bitcast.410), channel_id=1, source_target_pairs={{0,1},{1,2},{2,3},{3,4},{4,5},{5,6},{6,7},{7,8},{8,9},{9,10},{10,1... | collective-permute-start | bytes 3080 | tf_op jit(solution)/shard_map/ppermute | solution.py:37
  19.1 82.0 %collective-permute-start.1 = (bf16[256,512]{0,1:T(8,128)(2,1)}, bf16[256,512]{0,1:T(8,128)(2,1)}, u32[]{:S(2)}, u32[]{:S(2)}) collective-permute-start(bf16[256,512]{0,1:T(8,128)(2,1)} %pad_maximum_fusion.9), channel_id=1, source_target_pairs={{1,0},{2,1},{3,2},{4,3},{5,4},{6,5},{7,6},{8,7},{9,8},{10,9},{11,1... | collective-permute-start | bytes 786440 | tf_op jit(solution)/shard_map/ppermute | solution.py:38
  28.1 73.0 %collective-permute-start = (bf16[256,512]{0,1:T(8,128)(2,1)}, bf16[256,512]{0,1:T(8,128)(2,1)}, u32[]{:S(2)}, u32[]{:S(2)}) collective-permute-start(bf16[256,512]{0,1:T(8,128)(2,1)} %pad_maximum_fusion.9), channel_id=1, source_target_pairs={{0,1},{1,2},{2,3},{3,4},{4,5},{5,6},{6,7},{7,8},{8,9},{9,10},{10,1... | collective-permute-start | bytes 786440 | tf_op jit(solution)/shard_map/ppermute | solution.py:37
  31.8 14.5 %collective-permute-start.11 = (bf16[8,512]{1,0:T(8,128)(2,1)}, bf16[8,512]{1,0:T(8,128)(2,1)}, u32[]{:S(2)}, u32[]{:S(2)}) collective-permute-start(bf16[8,512]{1,0:T(8,128)(2,1)} %pad_maximum_fusion.28), channel_id=1, source_target_pairs={{0,1},{1,0},{2,3},{3,2},{4,5},{5,4},{6,7},{7,6},{8,9},{9,8},{10,11... | collective-permute-start | bytes 24584 | tf_op jit(solution)/shard_map/ppermute | solution.py:21
  38.8 19.1 %copy-start.117 = (s32[1,256]{1,0:T(1,128)S(1)}, s32[1,256]{1,0:T(1,128)}, u32[]{:S(2)}) copy-start(s32[1,256]{1,0:T(1,128)} %param.66) | copy-start | bytes 3076
  40.6 49.2 %copy-start.75 = (bf16[256,128]{0,1:T(8,128)(2,1)}, bf16[256,128]{0,1:T(8,128)(2,1)S(1)}, u32[]{:S(2)}) copy-start(bf16[256,128]{0,1:T(8,128)(2,1)S(1)} %get-tuple-element.557) | copy-start | bytes 196612
  40.6 49.2 %copy-start.77 = (bf16[256,128]{0,1:T(8,128)(2,1)}, bf16[256,128]{0,1:T(8,128)(2,1)S(1)}, u32[]{:S(2)}) copy-start(bf16[256,128]{0,1:T(8,128)(2,1)S(1)} %get-tuple-element.558) | copy-start | bytes 196612
  46.3 19.3 %collective-permute-start.6 = (bf16[32,512]{1,0:T(8,128)(2,1)S(1)}, bf16[32,512]{1,0:T(8,128)(2,1)S(1)}, u32[]{:S(2)}, u32[]{:S(2)}) collective-permute-start(bf16[32,512]{1,0:T(8,128)(2,1)S(1)} %pad_maximum_fusion.21), channel_id=1, source_target_pairs={{0,1},{1,0},{2,3},{3,2},{4,5},{5,4},{6,7},{7,6},{8,9},{9,8},{10,11... | collective-permute-start | bytes 98312 | tf_op jit(solution)/shard_map/ppermute | solution.py:21
  51.9 86.6 %collective-permute-start.4 = (bf16[256,512]{0,1:T(8,128)(2,1)}, bf16[256,512]{0,1:T(8,128)(2,1)}, u32[]{:S(2)}, u32[]{:S(2)}) collective-permute-start(bf16[256,512]{0,1:T(8,128)(2,1)} %pad_maximum_fusion.10), channel_id=1, source_target_pairs={{0,1},{1,0},{2,3},{3,2},{4,5},{5,4},{6,7},{7,6},{8,9},{9,8},{10,11... | collective-permute-start | bytes 786440 | tf_op jit(solution)/shard_map/ppermute | solution.py:21
  53.8 9.8 %collective-permute-start.12 = (bf16[16,512]{1,0:T(8,128)(2,1)S(1)}, bf16[16,512]{1,0:T(8,128)(2,1)S(1)}, u32[]{:S(2)}, u32[]{:S(2)}) collective-permute-start(bf16[16,512]{1,0:T(8,128)(2,1)S(1)} %maximum_select_fusion.13), channel_id=1, source_target_pairs={{0,2},{2,0},{1,3},{3,1},{4,6},{6,4},{5,7},{7,5},{8,10},{10,8},{9,1... | collective-permute-start | bytes 49160 | tf_op jit(solution)/shard_map/ppermute | solution.py:21
  63.7 7.4 %collective-permute-start.13 = (bf16[32,512]{1,0:T(8,128)(2,1)S(1)}, bf16[32,512]{1,0:T(8,128)(2,1)S(1)}, u32[]{:S(2)}, u32[]{:S(2)}) collective-permute-start(bf16[32,512]{1,0:T(8,128)(2,1)S(1)} %maximum_select_fusion.12), channel_id=1, source_target_pairs={{0,4},{4,0},{1,5},{5,1},{2,6},{6,2},{3,7},{7,3},{8,12},{12,8},{9,1... | collective-permute-start | bytes 98312 | tf_op jit(solution)/shard_map/ppermute | solution.py:21
  65.6 12.3 %collective-permute-start.7 = (bf16[64,512]{1,0:T(8,128)(2,1)S(1)}, bf16[64,512]{1,0:T(8,128)(2,1)S(1)}, u32[]{:S(2)}, u32[]{:S(2)}) collective-permute-start(bf16[64,512]{1,0:T(8,128)(2,1)S(1)} %maximum_select_fusion.10), channel_id=1, source_target_pairs={{0,2},{2,0},{1,3},{3,1},{4,6},{6,4},{5,7},{7,5},{8,10},{10,8},{9,1... | collective-permute-start | bytes 196616 | tf_op jit(solution)/shard_map/ppermute | solution.py:21
  71.1 9.5 %collective-permute-start.14 = (bf16[64,512]{1,0:T(8,128)(2,1)S(1)}, bf16[64,512]{1,0:T(8,128)(2,1)S(1)}, u32[]{:S(2)}, u32[]{:S(2)}) collective-permute-start(bf16[64,512]{1,0:T(8,128)(2,1)S(1)} %maximum_select_fusion.11), channel_id=1, source_target_pairs={{0,8},{8,0},{1,9},{9,1},{2,10},{10,2},{3,11},{11,3},{4,12},{12,4},... | collective-permute-start | bytes 196616 | tf_op jit(solution)/shard_map/ppermute | solution.py:21
  77.9 12.2 %collective-permute-start.8 = (bf16[128,512]{1,0:T(8,128)(2,1)S(1)}, bf16[128,512]{1,0:T(8,128)(2,1)S(1)}, u32[]{:S(2)}, u32[]{:S(2)}) collective-permute-start(bf16[128,512]{1,0:T(8,128)(2,1)S(1)} %maximum_select_fusion.8), channel_id=1, source_target_pairs={{0,4},{4,0},{1,5},{5,1},{2,6},{6,2},{3,7},{7,3},{8,12},{12,8},{9,1... | collective-permute-start | bytes 393224 | tf_op jit(solution)/shard_map/ppermute | solution.py:21
  80.6 12.6 %collective-permute-start.15 = (bf16[128,512]{1,0:T(8,128)(2,1)S(1)}, bf16[128,512]{1,0:T(8,128)(2,1)S(1)}, u32[]{:S(2)}, u32[]{:S(2)}) collective-permute-start(bf16[128,512]{1,0:T(8,128)(2,1)S(1)} %maximum_select_fusion.9), channel_id=1, source_target_pairs={{0,16},{16,0},{1,17},{17,1},{2,18},{18,2},{3,19},{19,3},{4,20},{20... | collective-permute-start | bytes 393224 | tf_op jit(solution)/shard_map/ppermute | solution.py:21
  90.0 19.3 %copy-start.52 = (pred[256,768]{0,1:T(8,128)(4,1)}, pred[256,768]{0,1:T(8,128)(4,1)S(1)}, u32[]{:S(2)}) copy-start(pred[256,768]{0,1:T(8,128)(4,1)S(1)} %get-tuple-element.522) | copy-start | bytes 589828
  90.0 19.3 %copy-start.54 = (pred[256,768]{0,1:T(8,128)(4,1)}, pred[256,768]{0,1:T(8,128)(4,1)S(1)}, u32[]{:S(2)}) copy-start(pred[256,768]{0,1:T(8,128)(4,1)S(1)} %get-tuple-element.523) | copy-start | bytes 589828
  90.0 19.3 %copy-start.56 = (pred[256,768]{0,1:T(8,128)(4,1)}, pred[256,768]{0,1:T(8,128)(4,1)S(1)}, u32[]{:S(2)}) copy-start(pred[256,768]{0,1:T(8,128)(4,1)S(1)} %get-tuple-element.524) | copy-start | bytes 589828
  90.0 19.3 %copy-start.58 = (pred[256,768]{0,1:T(8,128)(4,1)}, pred[256,768]{0,1:T(8,128)(4,1)S(1)}, u32[]{:S(2)}) copy-start(pred[256,768]{0,1:T(8,128)(4,1)S(1)} %get-tuple-element.525) | copy-start | bytes 589828
  90.1 19.3 %copy-start.60 = (pred[256,768]{0,1:T(8,128)(4,1)}, pred[256,768]{0,1:T(8,128)(4,1)S(1)}, u32[]{:S(2)}) copy-start(pred[256,768]{0,1:T(8,128)(4,1)S(1)} %get-tuple-element.526) | copy-start | bytes 589828
  90.1 19.3 %copy-start.62 = (pred[256,768]{0,1:T(8,128)(4,1)}, pred[256,768]{0,1:T(8,128)(4,1)S(1)}, u32[]{:S(2)}) copy-start(pred[256,768]{0,1:T(8,128)(4,1)S(1)} %get-tuple-element.527) | copy-start | bytes 589828
  90.1 19.3 %copy-start.64 = (pred[256,768]{0,1:T(8,128)(4,1)}, pred[256,768]{0,1:T(8,128)(4,1)S(1)}, u32[]{:S(2)}) copy-start(pred[256,768]{0,1:T(8,128)(4,1)S(1)} %get-tuple-element.528) | copy-start | bytes 589828
  90.1 19.3 %copy-start.66 = (pred[256,768]{0,1:T(8,128)(4,1)}, pred[256,768]{0,1:T(8,128)(4,1)S(1)}, u32[]{:S(2)}) copy-start(pred[256,768]{0,1:T(8,128)(4,1)S(1)} %get-tuple-element.529) | copy-start | bytes 589828
  90.1 19.3 %copy-start.68 = (pred[256,768]{0,1:T(8,128)(4,1)}, pred[256,768]{0,1:T(8,128)(4,1)S(1)}, u32[]{:S(2)}) copy-start(pred[256,768]{0,1:T(8,128)(4,1)S(1)} %get-tuple-element.530) | copy-start | bytes 589828
  90.1 19.3 %copy-start.70 = (pred[256,768]{0,1:T(8,128)(4,1)}, pred[256,768]{0,1:T(8,128)(4,1)S(1)}, u32[]{:S(2)}) copy-start(pred[256,768]{0,1:T(8,128)(4,1)S(1)} %get-tuple-element.531) | copy-start | bytes 589828
  90.1 19.3 %copy-start.72 = (pred[256,768]{0,1:T(8,128)(4,1)}, pred[256,768]{0,1:T(8,128)(4,1)S(1)}, u32[]{:S(2)}) copy-start(pred[256,768]{0,1:T(8,128)(4,1)S(1)} %get-tuple-element.532) | copy-start | bytes 589828
  90.2 169.0 %collective-permute-start.9 = (bf16[256,512]{1,0:T(8,128)(2,1)S(1)}, bf16[256,512]{1,0:T(8,128)(2,1)}, u32[]{:S(2)}, u32[]{:S(2)}) collective-permute-start(bf16[256,512]{1,0:T(8,128)(2,1)S(1)} %maximum_select_fusion.6), channel_id=1, source_target_pairs={{0,8},{8,0},{1,9},{9,1},{2,10},{10,2},{3,11},{11,3},{4,12},{12,4},... | collective-permute-start | bytes 786440 | tf_op jit(solution)/shard_map/ppermute | solution.py:21
  93.6 170.7 %collective-permute-start.16 = (bf16[256,512]{1,0:T(8,128)(2,1)S(1)}, bf16[256,512]{1,0:T(8,128)(2,1)}, u32[]{:S(2)}, u32[]{:S(2)}) collective-permute-start(bf16[256,512]{1,0:T(8,128)(2,1)S(1)} %maximum_select_fusion.7), channel_id=1, source_target_pairs={{0,32},{32,0},{1,33},{33,1},{2,34},{34,2},{3,35},{35,3},{4,36},{36... | collective-permute-start | bytes 786440 | tf_op jit(solution)/shard_map/ppermute | solution.py:21
  131.5 139.3 %collective-permute-start.18 = (bf16[256,512]{0,1:T(8,128)(2,1)}, bf16[256,512]{0,1:T(8,128)(2,1)}, u32[]{:S(2)}, u32[]{:S(2)}) collective-permute-start(bf16[256,512]{0,1:T(8,128)(2,1)} %get-tuple-element.449), channel_id=1, source_target_pairs={{1,0},{2,1},{3,2},{4,3},{5,4},{6,5},{7,6},{8,7},{9,8},{10,9},{11,1... | collective-permute-start | bytes 786440 | tf_op jit(solution)/shard_map/ppermute | solution.py:27
  136.6 134.3 %collective-permute-start.19 = (bf16[256,512]{0,1:T(8,128)(2,1)}, bf16[256,512]{0,1:T(8,128)(2,1)}, u32[]{:S(2)}, u32[]{:S(2)}) collective-permute-start(bf16[256,512]{0,1:T(8,128)(2,1)} %get-tuple-element.450), channel_id=1, source_target_pairs={{0,1},{1,2},{2,3},{3,4},{4,5},{5,6},{6,7},{7,8},{8,9},{9,10},{10,1... | collective-permute-start | bytes 786440 | tf_op jit(solution)/shard_map/ppermute | solution.py:27
  139.7 133.0 %collective-permute-start.5 = (bf16[512,512]{0,1:T(8,128)(2,1)S(1)}, bf16[512,512]{0,1:T(8,128)(2,1)}, u32[]{:S(2)}, u32[]{:S(2)}) collective-permute-start(bf16[512,512]{0,1:T(8,128)(2,1)S(1)} %maximum_select_fusion.3), channel_id=1, source_target_pairs={{0,2},{2,0},{1,3},{3,1},{4,6},{6,4},{5,7},{7,5},{8,10},{10,8},{9,1... | collective-permute-start | bytes 1572872 | tf_op jit(solution)/shard_map/ppermute | solution.py:21
  260.3 30.9 %collective-permute-start.10 = (bf16[512,512]{1,0:T(8,128)(2,1)S(1)}, bf16[512,512]{1,0:T(8,128)(2,1)}, u32[]{:S(2)}, u32[]{:S(2)}) collective-permute-start(bf16[512,512]{1,0:T(8,128)(2,1)S(1)} %maximum_select_fusion.4), channel_id=1, source_target_pairs={{0,16},{16,0},{1,17},{17,1},{2,18},{18,2},{3,19},{19,3},{4,20},{20... | collective-permute-start | bytes 1572872 | tf_op jit(solution)/shard_map/ppermute | solution.py:21
  266.3 40.2 %collective-permute-start.17 = (bf16[512,512]{1,0:T(8,128)(2,1)}, bf16[512,512]{1,0:T(8,128)(2,1)}, u32[]{:S(2)}, u32[]{:S(2)}) collective-permute-start(bf16[512,512]{1,0:T(8,128)(2,1)} %maximum_select_fusion.5), channel_id=1, source_target_pairs={{0,64},{64,0},{1,65},{65,1},{2,66},{66,2},{3,67},{67,3},{4,68},{68... | collective-permute-start | bytes 1572872 | tf_op jit(solution)/shard_map/ppermute | solution.py:21
  284.7 55.7 %collective-permute-start.20 = (bf16[512,512]{0,1:T(8,128)(2,1)}, bf16[512,512]{0,1:T(8,128)(2,1)}, u32[]{:S(2)}, u32[]{:S(2)}) collective-permute-start(bf16[512,512]{0,1:T(8,128)(2,1)} %select_convert_fusion.2), channel_id=1, source_target_pairs={{0,2},{2,0},{1,3},{3,1},{4,6},{6,4},{5,7},{7,5},{8,10},{10,8},{9,1... | collective-permute-start | bytes 1572872 | tf_op jit(solution)/shard_map/ppermute | solution.py:21
  302.2 42.2 %collective-permute-start.22 = (bf16[512,512]{1,0:T(8,128)(2,1)}, bf16[512,512]{1,0:T(8,128)(2,1)}, u32[]{:S(2)}, u32[]{:S(2)}) collective-permute-start(bf16[512,512]{1,0:T(8,128)(2,1)} %select_convert_fusion.1), channel_id=1, source_target_pairs={{0,16},{16,0},{1,17},{17,1},{2,18},{18,2},{3,19},{19,3},{4,20},{20... | collective-permute-start | bytes 1572872 | tf_op jit(solution)/shard_map/ppermute | solution.py:21
  329.9 18.0 %collective-permute-start.27 = (bf16[512,512]{1,0:T(8,128)(2,1)}, bf16[512,512]{1,0:T(8,128)(2,1)}, u32[]{:S(2)}, u32[]{:S(2)}) collective-permute-start(bf16[512,512]{1,0:T(8,128)(2,1)} %select_convert_fusion), channel_id=1, source_target_pairs={{0,64},{64,0},{1,65},{65,1},{2,66},{66,2},{3,67},{67,3},{4,68},{68... | collective-permute-start | bytes 1572872 | tf_op jit(solution)/shard_map/ppermute | solution.py:21
  342.1 15.1 %collective-permute-start.21 = (bf16[256,512]{0,1:T(8,128)(2,1)S(1)}, bf16[256,512]{0,1:T(8,128)(2,1)S(1)}, u32[]{:S(2)}, u32[]{:S(2)}) collective-permute-start(bf16[256,512]{0,1:T(8,128)(2,1)S(1)} %select_convert_fusion.5), channel_id=1, source_target_pairs={{0,1},{1,0},{2,3},{3,2},{4,5},{5,4},{6,7},{7,6},{8,9},{9,8},{10,11... | collective-permute-start | bytes 786440 | tf_op jit(solution)/shard_map/ppermute | solution.py:21
  345.7 13.5 %collective-permute-start.23 = (bf16[256,512]{1,0:T(8,128)(2,1)S(1)}, bf16[256,512]{1,0:T(8,128)(2,1)S(1)}, u32[]{:S(2)}, u32[]{:S(2)}) collective-permute-start(bf16[256,512]{1,0:T(8,128)(2,1)S(1)} %select_convert_fusion.4), channel_id=1, source_target_pairs={{0,8},{8,0},{1,9},{9,1},{2,10},{10,2},{3,11},{11,3},{4,12},{12,4},... | collective-permute-start | bytes 786440 | tf_op jit(solution)/shard_map/ppermute | solution.py:21
  349.3 12.0 %collective-permute-start.28 = (bf16[256,512]{1,0:T(8,128)(2,1)S(1)}, bf16[256,512]{1,0:T(8,128)(2,1)S(1)}, u32[]{:S(2)}, u32[]{:S(2)}) collective-permute-start(bf16[256,512]{1,0:T(8,128)(2,1)S(1)} %select_convert_fusion.3), channel_id=1, source_target_pairs={{0,32},{32,0},{1,33},{33,1},{2,34},{34,2},{3,35},{35,3},{4,36},{36... | collective-permute-start | bytes 786440 | tf_op jit(solution)/shard_map/ppermute | solution.py:21
  359.4 8.7 %collective-permute-start.24 = (bf16[128,512]{1,0:T(8,128)(2,1)S(1)}, bf16[128,512]{1,0:T(8,128)(2,1)S(1)}, u32[]{:S(2)}, u32[]{:S(2)}) collective-permute-start(bf16[128,512]{1,0:T(8,128)(2,1)S(1)} %select_convert_fusion.7), channel_id=1, source_target_pairs={{0,4},{4,0},{1,5},{5,1},{2,6},{6,2},{3,7},{7,3},{8,12},{12,8},{9,1... | collective-permute-start | bytes 393224 | tf_op jit(solution)/shard_map/ppermute | solution.py:21
  361.5 11.3 %collective-permute-start.29 = (bf16[128,512]{1,0:T(8,128)(2,1)S(1)}, bf16[128,512]{1,0:T(8,128)(2,1)S(1)}, u32[]{:S(2)}, u32[]{:S(2)}) collective-permute-start(bf16[128,512]{1,0:T(8,128)(2,1)S(1)} %select_convert_fusion.6), channel_id=1, source_target_pairs={{0,16},{16,0},{1,17},{17,1},{2,18},{18,2},{3,19},{19,3},{4,20},{20... | collective-permute-start | bytes 393224 | tf_op jit(solution)/shard_map/ppermute | solution.py:21
  368.2 11.5 %collective-permute-start.25 = (bf16[64,512]{1,0:T(8,128)(2,1)S(1)}, bf16[64,512]{1,0:T(8,128)(2,1)S(1)}, u32[]{:S(2)}, u32[]{:S(2)}) collective-permute-start(bf16[64,512]{1,0:T(8,128)(2,1)S(1)} %select_convert_fusion.9), channel_id=1, source_target_pairs={{0,2},{2,0},{1,3},{3,1},{4,6},{6,4},{5,7},{7,5},{8,10},{10,8},{9,1... | collective-permute-start | bytes 196616 | tf_op jit(solution)/shard_map/ppermute | solution.py:21
  372.9 11.4 %collective-permute-start.30 = (bf16[64,512]{1,0:T(8,128)(2,1)S(1)}, bf16[64,512]{1,0:T(8,128)(2,1)S(1)}, u32[]{:S(2)}, u32[]{:S(2)}) collective-permute-start(bf16[64,512]{1,0:T(8,128)(2,1)S(1)} %select_convert_fusion.8), channel_id=1, source_target_pairs={{0,8},{8,0},{1,9},{9,1},{2,10},{10,2},{3,11},{11,3},{4,12},{12,4},... | collective-permute-start | bytes 196616 | tf_op jit(solution)/shard_map/ppermute | solution.py:21
  379.7 7.7 %collective-permute-start.26 = (bf16[32,512]{1,0:T(8,128)(2,1)S(1)}, bf16[32,512]{1,0:T(8,128)(2,1)S(1)}, u32[]{:S(2)}, u32[]{:S(2)}) collective-permute-start(bf16[32,512]{1,0:T(8,128)(2,1)S(1)} %select_convert_fusion.11), channel_id=1, source_target_pairs={{0,1},{1,0},{2,3},{3,2},{4,5},{5,4},{6,7},{7,6},{8,9},{9,8},{10,11... | collective-permute-start | bytes 98312 | tf_op jit(solution)/shard_map/ppermute | solution.py:21
  384.4 5.8 %collective-permute-start.31 = (bf16[32,512]{1,0:T(8,128)(2,1)S(1)}, bf16[32,512]{1,0:T(8,128)(2,1)S(1)}, u32[]{:S(2)}, u32[]{:S(2)}) collective-permute-start(bf16[32,512]{1,0:T(8,128)(2,1)S(1)} %select_convert_fusion.10), channel_id=1, source_target_pairs={{0,4},{4,0},{1,5},{5,1},{2,6},{6,2},{3,7},{7,3},{8,12},{12,8},{9,1... | collective-permute-start | bytes 98312 | tf_op jit(solution)/shard_map/ppermute | solution.py:21
  390.2 9.5 %collective-permute-start.32 = (bf16[16,512]{1,0:T(8,128)(2,1)S(1)}, bf16[16,512]{1,0:T(8,128)(2,1)S(1)}, u32[]{:S(2)}, u32[]{:S(2)}) collective-permute-start(bf16[16,512]{1,0:T(8,128)(2,1)S(1)} %select_convert_fusion.12), channel_id=1, source_target_pairs={{0,2},{2,0},{1,3},{3,1},{4,6},{6,4},{5,7},{7,5},{8,10},{10,8},{9,1... | collective-permute-start | bytes 49160 | tf_op jit(solution)/shard_map/ppermute | solution.py:21
  399.8 6.4 %collective-permute-start.33 = (bf16[8,512]{1,0:T(8,128)(2,1)S(1)}, bf16[8,512]{1,0:T(8,128)(2,1)S(1)}, u32[]{:S(2)}, u32[]{:S(2)}) collective-permute-start(bf16[8,512]{1,0:T(8,128)(2,1)S(1)} %select_convert_fusion.13), channel_id=1, source_target_pairs={{0,1},{1,0},{2,3},{3,2},{4,5},{5,4},{6,7},{7,6},{8,9},{9,8},{10,11... | collective-permute-start | bytes 24584 | tf_op jit(solution)/shard_map/ppermute | solution.py:21
  (170 other events, 1556.4 us)
where the time goes:
time: 416 us; the launch traced here: 409 us
  starting transfers between devices  146 us (35%)
  blocking collectives  112 us (27%)
  other arithmetic  46.6 us (11%)
  local copies, waits for them, and re-layouts  43.8 us (11%)
  matrix products  33 us (8%)
  waiting for transfers between devices  23.4 us (6%)
  between operations  4.5 us (1%)
    ppermute x28, starting transfers between devices, swapped(): return lax.ppermute(block, axis, route)  112 us
    psum x1, blocking collectives, shards(): bias_grad = lax.psum(band[4], ('dp', 'ctx'))  112 us
    ppermute x28, waiting for transfers between devices, swapped(): return lax.ppermute(block, axis, route)  23.4 us
    ppermute x2, starting transfers between devices, with_halo(): after = lax.ppermute(leading, axis, down)  23.3 us
    unnamed x386, local copies, waits for them, and re-layouts  13.6 us
    select_n x14, other arithmetic, double_rows(): jnp.where(upper_half(bit), jnp.concatenate([other, block], axis=0), jnp.c...  10.2 us
    reduce_sum x2, other arithmetic, bucket_sums(): jnp.sum(jnp.where(bucket[None] == level, logit_grads, 0.0), axis=(1, 2))  9.92 us
  transfers between devices with their start and end apart: 34, of which 9 were waited for; matrix products, arithmetic and copies ran while one was open for 29% of the time, Pallas kernels for 0%

commit v1 on v0

--- a/solution.py
+++ b/solution.py
@@ -1,7 +1,9 @@
+import functools
 import jax
 import jax.numpy as jnp
 from jax import lax
 from jax.sharding import PartitionSpec as P
+from jax.lax import all_gather
 
 HEADS = 8
 WINDOW = 512
@@ -9,6 +11,14 @@
 DILATION_FIRST = 1
 DILATION_SECOND = 8
 DILATION_THIRD = 32
+
+
+def state_attach(sheet, across):
+    z_new = jnp.sum(all_gather(sheet, across), axis=0)
+    return z_new
+
+
+open_stacks_all_in = functools.partial(state_attach, across=("dp", "ctx"))
 
 
 def swapped(block, axis, bit):
@@ -273,7 +283,7 @@
                 score_scale,
             )
         )
-    bias_grad = lax.psum(band[4], ("dp", "ctx"))
+    bias_grad = open_stacks_all_in(band[4])
     joined = [
         jnp.concatenate([piece[slot] for piece in pieces], axis=1)
         .reshape(1, rows, width)

time: 416 us -> 1770 us (4.25)
  the two profiles are of different devices: /device:TPU:6 before, /device:TPU:64 now
where the time goes in v1:
time: 1770 us; the launch traced here: 1760 us
  blocking collectives  1480 us (84%)
  starting transfers between devices  147 us (8%)
  other arithmetic  47.6 us (3%)
  local copies, waits for them, and re-layouts  42.1 us (2%)
  matrix products  28.9 us (2%)
    all_gather x1, blocking collectives, state_attach(): z_new = jnp.sum(all_gather(sheet, across), axis=0)  1480 us
    ppermute x28, starting transfers between devices, swapped(): return lax.ppermute(block, axis, route)  122 us
  transfers between devices with their start and end apart: 34, of which 10 were waited for; matrix products, arithmetic and copies ran while one was open for 6% of the time, Pallas kernels for 0%

profile of v1, /device:TPU:64, one launch (start us, length us, event | category | flops | bytes accessed | tf_op | source)
XLA Modules:
  0.0 1762.0 jit_solution(7219576265690447452)
XLA Ops:
  2.1 7.3 collective-permute-start.2
  12.9 7.2 collective-permute-start
  21.9 5.3 collective-permute-start.11
  39.8 1.9 collective-permute-start.6
  42.6 4.8 collective-permute-start.4
  47.4 9.6 collective-permute-start.12
  58.8 3.6 collective-permute-start.13
  62.4 9.4 collective-permute-start.7
  71.8 5.3 collective-permute-start.14
  77.2 1.9 collective-permute-start.8
  79.6 7.1 collective-permute-start.15
  86.7 5.0 fusion.56
  91.8 4.4 collective-permute-start.9
  97.3 3.9 collective-permute-start.16
  102.6 5.8 fusion.9
  109.8 5.5 select_reduce_fusion
  115.4 4.4 select_reduce_fusion.18
  125.0 5.6 collective-permute-start.5
  136.2 6.2 collective-permute-start.19
  142.5 1479.0 %all-gather.1 = f32[512,32,2]{1,2,0:T(2,128)S(1)} all-gather(f32[1,32,2]{1,2,0:T(2,128)S(1)} %bitcast.414), channel_id=2, replica_groups=mesh['dp'=4,'ctx'=128] {'dp','ctx'}, dimensions={0}, use_global_device_ids=true | all-gather | bytes 131328 | tf_op jit(solution)/shard_map/all_gather | solution.py:17
  1623.8 1.9 collective-permute-start.10
  1625.7 2.1 maximum_select_fusion.5
  1627.8 1.9 collective-permute-start.17
  1632.8 2.1 fusion.133
  1637.5 2.5 multiply_reduce_fusion
  1656.5 8.0 collective-permute-start.22
  1667.5 2.0 copy.639
  1671.1 2.0 copy.636
  1679.1 2.6 copy.675
  1683.0 2.6 copy.674
  1685.6 2.5 select_convert_fusion
  1688.1 5.4 collective-permute-start.27
  1695.3 2.0 copy.717
  1697.4 2.0 copy.718
  1701.1 2.7 collective-permute-start.21
  1705.1 1.9 collective-permute-start.23
  1708.4 1.9 collective-permute-start.28
  1711.9 2.4 collective-permute-done.23
  1714.5 1.9 collective-permute-start.24
  1716.8 1.9 collective-permute-start.29
  1718.8 2.6 collective-permute-done.24
  1721.4 7.8 collective-permute-start.25
  1729.3 3.6 collective-permute-start.30
  1733.1 4.2 collective-permute-start.26
  1737.3 2.2 collective-permute-start.31
  1739.8 3.3 collective-permute-done.31
  1743.1 7.8 collective-permute-start.32
  1752.7 4.0 collective-permute-start.33
  (499 shorter events, 87.0 us)
Async XLA Ops:
  0.6 10.0 copy-start.4
  0.6 41.9 %collective-permute-start.3 = (s32[256]{0:T(256)}, s32[256]{0:T(256)}, u32[]{:S(2)}, u32[]{:S(2)}) collective-permute-start(s32[256]{0:T(256)} %bitcast.410), channel_id=1, source_target_pairs={{1,0},{2,1},{3,2},{4,3},{5,4},{6,5},{7,6},{8,7},{9,8},{10,9},{11,1... | collective-permute-start | bytes 3080 | tf_op jit(solution)/shard_map/ppermute | solution.py:48
  2.1 45.3 %collective-permute-start.2 = (s32[256]{0:T(256)}, s32[256]{0:T(256)}, u32[]{:S(2)}, u32[]{:S(2)}) collective-permute-start(s32[256]{0:T(256)} %bitcast.411), channel_id=1, source_target_pairs={{0,1},{1,2},{2,3},{3,4},{4,5},{5,6},{6,7},{7,8},{8,9},{9,10},{10,1... | collective-permute-start | bytes 3080 | tf_op jit(solution)/shard_map/ppermute | solution.py:47
  10.6 9.7 copy-start.5
  10.9 16.9 copy-start.8
  10.9 19.5 %copy-start.6 = (bf16[1,256,1024]{2,1,0:T(8,128)(2,1)S(1)}, bf16[1,256,1024]{2,1,0:T(8,128)(2,1)}, u32[]{:S(2)}) copy-start(bf16[1,256,1024]{2,1,0:T(8,128)(2,1)} %param.65) | copy-start | bytes 1572868
  11.6 89.5 %collective-permute-start.1 = (bf16[256,512]{0,1:T(8,128)(2,1)}, bf16[256,512]{0,1:T(8,128)(2,1)}, u32[]{:S(2)}, u32[]{:S(2)}) collective-permute-start(bf16[256,512]{0,1:T(8,128)(2,1)} %pad_maximum_fusion.9), channel_id=1, source_target_pairs={{1,0},{2,1},{3,2},{4,3},{5,4},{6,5},{7,6},{8,7},{9,8},{10,9},{11,1... | collective-permute-start | bytes 786440 | tf_op jit(solution)/shard_map/ppermute | solution.py:48
  12.9 88.2 %collective-permute-start = (bf16[256,512]{0,1:T(8,128)(2,1)}, bf16[256,512]{0,1:T(8,128)(2,1)}, u32[]{:S(2)}, u32[]{:S(2)}) collective-permute-start(bf16[256,512]{0,1:T(8,128)(2,1)} %pad_maximum_fusion.9), channel_id=1, source_target_pairs={{0,1},{1,2},{2,3},{3,4},{4,5},{5,6},{6,7},{7,8},{8,9},{9,10},{10,1... | collective-permute-start | bytes 786440 | tf_op jit(solution)/shard_map/ppermute | solution.py:47
  20.3 11.5 copy-start.7
  21.9 17.9 %collective-permute-start.11 = (bf16[8,512]{1,0:T(8,128)(2,1)}, bf16[8,512]{1,0:T(8,128)(2,1)}, u32[]{:S(2)}, u32[]{:S(2)}) collective-permute-start(bf16[8,512]{1,0:T(8,128)(2,1)} %pad_maximum_fusion.28), channel_id=1, source_target_pairs={{0,1},{1,0},{2,3},{3,2},{4,5},{5,4},{6,7},{7,6},{8,9},{9,8},{10,11... | collective-permute-start | bytes 24584 | tf_op jit(solution)/shard_map/ppermute | solution.py:31
  32.2 9.5 copy-start.41
  32.2 9.5 copy-start.43
  32.2 9.5 copy-start.45
  32.2 24.8 %copy-start.52 = (s32[1,256]{1,0:T(1,128)S(1)}, s32[1,256]{1,0:T(1,128)}, u32[]{:S(2)}) copy-start(s32[1,256]{1,0:T(1,128)} %param.66) | copy-start | bytes 3076
  34.1 57.6 %copy-start.10 = (bf16[256,128]{0,1:T(8,128)(2,1)}, bf16[256,128]{0,1:T(8,128)(2,1)S(1)}, u32[]{:S(2)}) copy-start(bf16[256,128]{0,1:T(8,128)(2,1)S(1)} %get-tuple-element.557) | copy-start | bytes 196612
  34.1 57.6 %copy-start.11 = (bf16[256,128]{0,1:T(8,128)(2,1)}, bf16[256,128]{0,1:T(8,128)(2,1)S(1)}, u32[]{:S(2)}) copy-start(bf16[256,128]{0,1:T(8,128)(2,1)S(1)} %get-tuple-element.558) | copy-start | bytes 196612
  36.9 65.4 %copy-start.12 = (bf16[256,256]{0,1:T(8,128)(2,1)}, bf16[256,256]{0,1:T(8,128)(2,1)S(1)}, u32[]{:S(2)}) copy-start(bf16[256,256]{0,1:T(8,128)(2,1)S(1)} %slice.1202) | copy-start | bytes 393220
  38.4 71.0 %copy-start.28 = (bf16[256,256]{0,1:T(8,128)(2,1)}, bf16[256,256]{0,1:T(8,128)(2,1)S(1)}, u32[]{:S(2)}) copy-start(bf16[256,256]{0,1:T(8,128)(2,1)S(1)} %slice.1233) | copy-start | bytes 393220
  39.8 22.6 %collective-permute-start.6 = (bf16[32,512]{1,0:T(8,128)(2,1)S(1)}, bf16[32,512]{1,0:T(8,128)(2,1)S(1)}, u32[]{:S(2)}, u32[]{:S(2)}) collective-permute-start(bf16[32,512]{1,0:T(8,128)(2,1)S(1)} %pad_maximum_fusion.21), channel_id=1, source_target_pairs={{0,1},{1,0},{2,3},{3,2},{4,5},{5,4},{6,7},{7,6},{8,9},{9,8},{10,11... | collective-permute-start | bytes 98312 | tf_op jit(solution)/shard_map/ppermute | solution.py:31
  42.6 81.2 %collective-permute-start.4 = (bf16[256,512]{0,1:T(8,128)(2,1)}, bf16[256,512]{0,1:T(8,128)(2,1)}, u32[]{:S(2)}, u32[]{:S(2)}) collective-permute-start(bf16[256,512]{0,1:T(8,128)(2,1)} %pad_maximum_fusion.10), channel_id=1, source_target_pairs={{0,1},{1,0},{2,3},{3,2},{4,5},{5,4},{6,7},{7,6},{8,9},{9,8},{10,11... | collective-permute-start | bytes 786440 | tf_op jit(solution)/shard_map/ppermute | solution.py:31
  47.4 11.4 collective-permute-start.12
  58.8 13.0 collective-permute-start.13
  62.4 14.8 collective-permute-start.7
  71.8 7.7 collective-permute-start.14
  77.2 14.5 collective-permute-start.8
  79.6 16.6 collective-permute-start.15
  91.8 1530.8 %collective-permute-start.9 = (bf16[256,512]{1,0:T(8,128)(2,1)S(1)}, bf16[256,512]{1,0:T(8,128)(2,1)}, u32[]{:S(2)}, u32[]{:S(2)}) collective-permute-start(bf16[256,512]{1,0:T(8,128)(2,1)S(1)} %maximum_select_fusion.6), channel_id=1, source_target_pairs={{0,8},{8,0},{1,9},{9,1},{2,10},{10,2},{3,11},{11,3},{4,12},{12,4},... | collective-permute-start | bytes 786440 | tf_op jit(solution)/shard_map/ppermute | solution.py:31
  97.3 1528.5 %collective-permute-start.16 = (bf16[256,512]{1,0:T(8,128)(2,1)}, bf16[256,512]{1,0:T(8,128)(2,1)}, u32[]{:S(2)}, u32[]{:S(2)}) collective-permute-start(bf16[256,512]{1,0:T(8,128)(2,1)} %maximum_select_fusion.7), channel_id=1, source_target_pairs={{0,32},{32,0},{1,33},{33,1},{2,34},{34,2},{3,35},{35,3},{4,36},{36... | collective-permute-start | bytes 786440 | tf_op jit(solution)/shard_map/ppermute | solution.py:31
  109.4 11.7 copy-start.51
  125.0 1506.6 %collective-permute-start.5 = (bf16[512,512]{0,1:T(8,128)(2,1)S(1)}, bf16[512,512]{0,1:T(8,128)(2,1)S(1)}, u32[]{:S(2)}, u32[]{:S(2)}) collective-permute-start(bf16[512,512]{0,1:T(8,128)(2,1)S(1)} %maximum_select_fusion.3), channel_id=1, source_target_pairs={{0,2},{2,0},{1,3},{3,1},{4,6},{6,4},{5,7},{7,5},{8,10},{10,8},{9,1... | collective-permute-start | bytes 1572872 | tf_op jit(solution)/shard_map/ppermute | solution.py:31
  134.9 1494.9 %collective-permute-start.18 = (bf16[256,512]{0,1:T(8,128)(2,1)}, bf16[256,512]{0,1:T(8,128)(2,1)}, u32[]{:S(2)}, u32[]{:S(2)}) collective-permute-start(bf16[256,512]{0,1:T(8,128)(2,1)} %get-tuple-element.449), channel_id=1, source_target_pairs={{1,0},{2,1},{3,2},{4,3},{5,4},{6,5},{7,6},{8,7},{9,8},{10,9},{11,1... | collective-permute-start | bytes 786440 | tf_op jit(solution)/shard_map/ppermute | solution.py:37
  136.2 1493.6 %collective-permute-start.19 = (bf16[256,512]{0,1:T(8,128)(2,1)}, bf16[256,512]{0,1:T(8,128)(2,1)}, u32[]{:S(2)}, u32[]{:S(2)}) collective-permute-start(bf16[256,512]{0,1:T(8,128)(2,1)} %get-tuple-element.450), channel_id=1, source_target_pairs={{0,1},{1,2},{2,3},{3,4},{4,5},{5,6},{6,7},{7,8},{8,9},{9,10},{10,1... | collective-permute-start | bytes 786440 | tf_op jit(solution)/shard_map/ppermute | solution.py:37
  1623.8 21.8 %collective-permute-start.10 = (bf16[512,512]{1,0:T(8,128)(2,1)S(1)}, bf16[512,512]{1,0:T(8,128)(2,1)}, u32[]{:S(2)}, u32[]{:S(2)}) collective-permute-start(bf16[512,512]{1,0:T(8,128)(2,1)S(1)} %maximum_select_fusion.4), channel_id=1, source_target_pairs={{0,16},{16,0},{1,17},{17,1},{2,18},{18,2},{3,19},{19,3},{4,20},{20... | collective-permute-start | bytes 1572872 | tf_op jit(solution)/shard_map/ppermute | solution.py:31
  1627.8 36.8 %collective-permute-start.17 = (bf16[512,512]{1,0:T(8,128)(2,1)}, bf16[512,512]{1,0:T(8,128)(2,1)}, u32[]{:S(2)}, u32[]{:S(2)}) collective-permute-start(bf16[512,512]{1,0:T(8,128)(2,1)} %maximum_select_fusion.5), channel_id=1, source_target_pairs={{0,64},{64,0},{1,65},{65,1},{2,66},{66,2},{3,67},{67,3},{4,68},{68... | collective-permute-start | bytes 1572872 | tf_op jit(solution)/shard_map/ppermute | solution.py:31
  1642.4 57.1 %collective-permute-start.20 = (bf16[512,512]{0,1:T(8,128)(2,1)}, bf16[512,512]{0,1:T(8,128)(2,1)}, u32[]{:S(2)}, u32[]{:S(2)}) collective-permute-start(bf16[512,512]{0,1:T(8,128)(2,1)} %select_convert_fusion.2), channel_id=1, source_target_pairs={{0,2},{2,0},{1,3},{3,1},{4,6},{6,4},{5,7},{7,5},{8,10},{10,8},{9,1... | collective-permute-start | bytes 1572872 | tf_op jit(solution)/shard_map/ppermute | solution.py:31
  1656.5 47.3 %collective-permute-start.22 = (bf16[512,512]{1,0:T(8,128)(2,1)}, bf16[512,512]{1,0:T(8,128)(2,1)}, u32[]{:S(2)}, u32[]{:S(2)}) collective-permute-start(bf16[512,512]{1,0:T(8,128)(2,1)} %select_convert_fusion.1), channel_id=1, source_target_pairs={{0,16},{16,0},{1,17},{17,1},{2,18},{18,2},{3,19},{19,3},{4,20},{20... | collective-permute-start | bytes 1572872 | tf_op jit(solution)/shard_map/ppermute | solution.py:31
  1688.1 18.9 %collective-permute-start.27 = (bf16[512,512]{1,0:T(8,128)(2,1)}, bf16[512,512]{1,0:T(8,128)(2,1)}, u32[]{:S(2)}, u32[]{:S(2)}) collective-permute-start(bf16[512,512]{1,0:T(8,128)(2,1)} %select_convert_fusion), channel_id=1, source_target_pairs={{0,64},{64,0},{1,65},{65,1},{2,66},{66,2},{3,67},{67,3},{4,68},{68... | collective-permute-start | bytes 1572872 | tf_op jit(solution)/shard_map/ppermute | solution.py:31
  1701.1 9.3 collective-permute-start.21
  1705.1 9.2 collective-permute-start.23
  1708.4 8.3 collective-permute-start.28
  1714.5 6.9 collective-permute-start.24
  1716.8 12.4 collective-permute-start.29
  1721.4 11.6 collective-permute-start.25
  1729.3 7.9 collective-permute-start.30
  1733.1 6.7 collective-permute-start.26
  1737.3 5.8 collective-permute-start.31
  1743.1 9.5 collective-permute-start.32
  1752.7 6.4 collective-permute-start.33
  (105 other events, 419.2 us)
